TPU v7x, 512 devices: a whole 4x4x16 slice. The times are simulated.
512 devices in a mesh: dp: 32 (over z_lo, x), fly: 16 (over z_hi, y, core).
Axes of the slice: x: 4, y: 4, z: 16 (z_hi: 2, z_lo: 8; z = z_hi * 8 + z_lo), core: 2. Of those that a mesh axis runs over, the one named last changes fastest.
Arguments:
- tokens: bfloat16 [4096, 8192], P('dp', 'fly'), may hold values from -6 to 6
- hidden_grad: bfloat16 [4096, 16384], P('dp', 'fly'), may hold values from -6 to 6
- w_up: bfloat16 [6, 256, 16384], P(None, 'dp', 'fly'), may hold values from -0.15625 to 0.15625
- pattern: int32 [6, 64], P(None, 'fly'), may hold values 0 or 1
Outputs:
- input_grad: bfloat16 [4096, 8192], P('dp', 'fly')
- weight_grad: float32 [6, 256, 16384], P(None, 'dp', 'fly')
Inputs may be any that keep to these rules, and one draw needn't show every extreme that they name: pattern[t, f] is 1 where block f of factor t is kept and 0 where it is dropped.
All inputs are finite; a program needn't handle non-finite values.
Results may differ from a plain program's by a relative error of at most 0.0049.
Values may be sent and summed in bfloat16 or wider, within the bound.
No kernel may reach another device: no remote copies, remote signals or barrier semaphores. Data moves between devices by JAX's collectives and lax.ppermute only.
A program may use at most 64 MiB of HBM per device.

v0:
```python
import jax
import jax.numpy as jnp
from jax import lax
from jax.sharding import PartitionSpec as P

BS = 256


def partner_2(block, axis, bit):
    count = lax.axis_size(axis)
    route = []
    for low in range(count):
        high = low | 1 << bit
        if high != low and high < count:
            route += [(low, high), (high, low)]
    return lax.ppermute(block, axis, route)


def shifted(value, axis, by):
    devices = lax.axis_size(axis)
    return lax.ppermute(value, axis, [(i, (i + by) % devices) for i in range(devices)])


def flip_blocks(values, stride):
    if stride == 0:
        return values
    row_count, block_count, inner_size = values.shape
    shaped = values.reshape(row_count, block_count // (2 * stride), 2, stride, inner_size)
    return shaped[:, :, ::-1].reshape(row_count, block_count, inner_size)


def stride_of(factor):
    return 0 if factor == 0 else 2 ** (factor - 1)


def pick_rows(stacked, index, replicas):
    return lax.dynamic_index_in_dim(stacked, index % replicas, 1, keepdims=False)


def body(tokens, hidden_grad, w_up, pattern):
    row_count, local_width = tokens.shape
    factor_count = w_up.shape[0]
    hidden_width = hidden_grad.shape[1]
    local_blocks = local_width // BS
    group_width = hidden_width // local_blocks
    weights = lax.all_gather(w_up, "dp", axis=1, tiled=True)
    keep_cols = jnp.broadcast_to(pattern[:, :, None], (factor_count, pattern.shape[1], BS)).reshape(
        factor_count, hidden_width
    )
    masked = (weights * keep_cols.astype(jnp.bfloat16)[:, None, :]).reshape(
        factor_count, BS, local_blocks, group_width
    )
    keep_f = keep_cols.astype(jnp.float32)
    token_blocks = tokens.reshape(row_count, local_blocks, BS)
    gathered = []
    for factor in range(factor_count):
        stride = stride_of(factor)
        if stride < local_blocks:
            gathered.append(flip_blocks(token_blocks, stride))
        else:
            bit_number = (stride // local_blocks).bit_length() - 1
            partner = partner_2(tokens, "fly", bit_number)
            gathered.append(partner.reshape(row_count, local_blocks, BS))
    pre_act = jnp.zeros((row_count, local_blocks, group_width), jnp.float32)
    for factor in range(factor_count):
        pre_act = pre_act + jnp.einsum(
            "ngb,bgc->ngc", gathered[factor], masked[factor], preferred_element_type=jnp.float32
        )
    squash = jax.nn.sigmoid(pre_act)
    derivative = squash * (1.0 + pre_act * (1.0 - squash))
    grad_pre = (
        hidden_grad.reshape(row_count, local_blocks, group_width).astype(jnp.float32) * derivative
    ).astype(jnp.bfloat16)
    input_total = jnp.zeros((row_count, local_blocks, BS), jnp.float32)
    for factor in range(factor_count):
        stride = stride_of(factor)
        contrib = jnp.einsum(
            "ngc,bgc->ngb", grad_pre, masked[factor], preferred_element_type=jnp.float32
        )
        if stride < local_blocks:
            input_total = input_total + flip_blocks(contrib, stride)
        else:
            bit_number = (stride // local_blocks).bit_length() - 1
            returned = partner_2(contrib.reshape(row_count, local_width), "fly", bit_number)
            input_total = input_total + returned.reshape(row_count, local_blocks, BS)
    input_grad = input_total.reshape(row_count, local_width).astype(jnp.bfloat16)
    replicas = lax.axis_size("dp")
    place = lax.axis_index("dp")
    row_share = BS // replicas
    terms = []
    for factor in range(factor_count):
        product_term = jnp.einsum(
            "ngb,ngc->bgc", gathered[factor], grad_pre, preferred_element_type=jnp.float32
        )
        terms.append(product_term.reshape(BS, hidden_width) * keep_f[factor][None, :])
    term_stack = jnp.stack(terms).reshape(factor_count, replicas, row_share, hidden_width)

    def turn_one(step, carry):
        return shifted(carry, "dp", 1) + pick_rows(
            term_stack, place - step - 2 + 2 * replicas, replicas
        )

    summed = lax.fori_loop(
        0, replicas - 1, turn_one, pick_rows(term_stack, place - 1 + replicas, replicas)
    )
    weight_grad = summed * (1.0 / replicas)
    return (input_grad, weight_grad)


def solution(mesh):
    return jax.shard_map(
        body,
        mesh=mesh,
        in_specs=(P("dp", "fly"), P("dp", "fly"), P(None, "dp", "fly"), P(None, "fly")),
        out_specs=(P("dp", "fly"), P(None, "dp", "fly")),
        check_vma=False,
    )
```

profile of v0, /device:TPU:8, one launch (start us, length us, event | category | flops | bytes accessed | tf_op | source)
XLA Modules:
  0.0 881.5 jit_solution(7239345191191575717)
XLA Ops:
  9.6 15.7 %collective-permute-start.4 = (bf16[128,512]{0,1:T(8,128)(2,1)}, bf16[128,512]{0,1:T(8,128)(2,1)}, u32[]{:S(2)}, u32[]{:S(2)}) collective-permute-start(bf16[128,512]{0,1:T(8,128)(2,1)} %copy.43), channel_id=1, source_target_pairs={{0,8},{8,0},{1,9},{9,1},{2,10},{10,2},{3,11},{11,3},{4,12},{12,4},... | collective-permute-start | bytes 393224 | tf_op jit(solution)/shard_map/ppermute | solution.py:16
  40.2 209.0 %all-gather.2.cloned.1.call-done = bf16[6,256,1024]{2,1,0:T(8,128)(2,1)} async-done(((bf16[6,8,1024]{2,1,0:T(8,128)(2,1)}), bf16[6,256,1024]{2,1,0:T(8,128)(2,1)}) %all-gather.2.cloned.1.call-update) | async-done | bytes 3145744 | tf_op jit(solution)/shard_map/all_gather | solution.py:46
  328.9 542.7 %while.17 = (s32[]{:T(128)}, f32[6,8,1024]{2,1,0:T(8,128)S(1)}, s32[]{:T(128)}, f32[6,32,8,1024]{3,2,1,0:T(8,128)}, s32[]{:T(128)}, /*index=5*/s32[]{:T(128)}, s32[]{:T(128)}, s32[]{:T(128)}, s32[]{:T(128)}) while((s32[]{:T(128)}, f32[6,8,1024]{2,1,0:T(8,128)S(1)}, s32[]{:T(128)}, f32[6,32,8,1024]{3,2,1,0:T(8,128)}, s32[]{:T(128)}, ...), condition=%wide.region_1.2_spmd, body=%wide.region_0.1_spmd.sunk | while | flops 49170 | bytes 1376560 | solution.py:103
  330.8 16.0 %collective-permute-done = f32[6,8,1024]{2,1,0:T(8,128)S(1)} collective-permute-done((f32[6,8,1024]{2,1,0:T(8,128)S(1)}, f32[6,8,1024]{2,1,0:T(8,128)S(1)}, u32[]{:S(2)}, u32[]{:S(2)}) %collective-permute-start) | collective-permute-done | bytes 196640 | tf_op jit(solution)/shard_map/while/body/eval_jaxpr/ppermute | solution.py:21
  349.7 15.1 %collective-permute-done = f32[6,8,1024]{2,1,0:T(8,128)S(1)} collective-permute-done((f32[6,8,1024]{2,1,0:T(8,128)S(1)}, f32[6,8,1024]{2,1,0:T(8,128)S(1)}, u32[]{:S(2)}, u32[]{:S(2)}) %collective-permute-start) | collective-permute-done | bytes 196640 | tf_op jit(solution)/shard_map/while/body/eval_jaxpr/ppermute | solution.py:21
  367.7 14.3 %collective-permute-done = f32[6,8,1024]{2,1,0:T(8,128)S(1)} collective-permute-done((f32[6,8,1024]{2,1,0:T(8,128)S(1)}, f32[6,8,1024]{2,1,0:T(8,128)S(1)}, u32[]{:S(2)}, u32[]{:S(2)}) %collective-permute-start) | collective-permute-done | bytes 196640 | tf_op jit(solution)/shard_map/while/body/eval_jaxpr/ppermute | solution.py:21
  385.0 14.3 %collective-permute-done = f32[6,8,1024]{2,1,0:T(8,128)S(1)} collective-permute-done((f32[6,8,1024]{2,1,0:T(8,128)S(1)}, f32[6,8,1024]{2,1,0:T(8,128)S(1)}, u32[]{:S(2)}, u32[]{:S(2)}) %collective-permute-start) | collective-permute-done | bytes 196640 | tf_op jit(solution)/shard_map/while/body/eval_jaxpr/ppermute | solution.py:21
  402.2 14.3 %collective-permute-done = f32[6,8,1024]{2,1,0:T(8,128)S(1)} collective-permute-done((f32[6,8,1024]{2,1,0:T(8,128)S(1)}, f32[6,8,1024]{2,1,0:T(8,128)S(1)}, u32[]{:S(2)}, u32[]{:S(2)}) %collective-permute-start) | collective-permute-done | bytes 196640 | tf_op jit(solution)/shard_map/while/body/eval_jaxpr/ppermute | solution.py:21
  419.4 14.3 %collective-permute-done = f32[6,8,1024]{2,1,0:T(8,128)S(1)} collective-permute-done((f32[6,8,1024]{2,1,0:T(8,128)S(1)}, f32[6,8,1024]{2,1,0:T(8,128)S(1)}, u32[]{:S(2)}, u32[]{:S(2)}) %collective-permute-start) | collective-permute-done | bytes 196640 | tf_op jit(solution)/shard_map/while/body/eval_jaxpr/ppermute | solution.py:21
  436.7 14.3 %collective-permute-done = f32[6,8,1024]{2,1,0:T(8,128)S(1)} collective-permute-done((f32[6,8,1024]{2,1,0:T(8,128)S(1)}, f32[6,8,1024]{2,1,0:T(8,128)S(1)}, u32[]{:S(2)}, u32[]{:S(2)}) %collective-permute-start) | collective-permute-done | bytes 196640 | tf_op jit(solution)/shard_map/while/body/eval_jaxpr/ppermute | solution.py:21
  453.9 14.3 %collective-permute-done = f32[6,8,1024]{2,1,0:T(8,128)S(1)} collective-permute-done((f32[6,8,1024]{2,1,0:T(8,128)S(1)}, f32[6,8,1024]{2,1,0:T(8,128)S(1)}, u32[]{:S(2)}, u32[]{:S(2)}) %collective-permute-start) | collective-permute-done | bytes 196640 | tf_op jit(solution)/shard_map/while/body/eval_jaxpr/ppermute | solution.py:21
  471.2 14.3 %collective-permute-done = f32[6,8,1024]{2,1,0:T(8,128)S(1)} collective-permute-done((f32[6,8,1024]{2,1,0:T(8,128)S(1)}, f32[6,8,1024]{2,1,0:T(8,128)S(1)}, u32[]{:S(2)}, u32[]{:S(2)}) %collective-permute-start) | collective-permute-done | bytes 196640 | tf_op jit(solution)/shard_map/while/body/eval_jaxpr/ppermute | solution.py:21
  488.4 14.3 %collective-permute-done = f32[6,8,1024]{2,1,0:T(8,128)S(1)} collective-permute-done((f32[6,8,1024]{2,1,0:T(8,128)S(1)}, f32[6,8,1024]{2,1,0:T(8,128)S(1)}, u32[]{:S(2)}, u32[]{:S(2)}) %collective-permute-start) | collective-permute-done | bytes 196640 | tf_op jit(solution)/shard_map/while/body/eval_jaxpr/ppermute | solution.py:21
  505.7 14.3 %collective-permute-done = f32[6,8,1024]{2,1,0:T(8,128)S(1)} collective-permute-done((f32[6,8,1024]{2,1,0:T(8,128)S(1)}, f32[6,8,1024]{2,1,0:T(8,128)S(1)}, u32[]{:S(2)}, u32[]{:S(2)}) %collective-permute-start) | collective-permute-done | bytes 196640 | tf_op jit(solution)/shard_map/while/body/eval_jaxpr/ppermute | solution.py:21
  522.9 14.3 %collective-permute-done = f32[6,8,1024]{2,1,0:T(8,128)S(1)} collective-permute-done((f32[6,8,1024]{2,1,0:T(8,128)S(1)}, f32[6,8,1024]{2,1,0:T(8,128)S(1)}, u32[]{:S(2)}, u32[]{:S(2)}) %collective-permute-start) | collective-permute-done | bytes 196640 | tf_op jit(solution)/shard_map/while/body/eval_jaxpr/ppermute | solution.py:21
  557.4 15.2 %collective-permute-done = f32[6,8,1024]{2,1,0:T(8,128)S(1)} collective-permute-done((f32[6,8,1024]{2,1,0:T(8,128)S(1)}, f32[6,8,1024]{2,1,0:T(8,128)S(1)}, u32[]{:S(2)}, u32[]{:S(2)}) %collective-permute-start) | collective-permute-done | bytes 196640 | tf_op jit(solution)/shard_map/while/body/eval_jaxpr/ppermute | solution.py:21
  575.5 16.3 %collective-permute-done = f32[6,8,1024]{2,1,0:T(8,128)S(1)} collective-permute-done((f32[6,8,1024]{2,1,0:T(8,128)S(1)}, f32[6,8,1024]{2,1,0:T(8,128)S(1)}, u32[]{:S(2)}, u32[]{:S(2)}) %collective-permute-start) | collective-permute-done | bytes 196640 | tf_op jit(solution)/shard_map/while/body/eval_jaxpr/ppermute | solution.py:21
  594.7 15.6 %collective-permute-done = f32[6,8,1024]{2,1,0:T(8,128)S(1)} collective-permute-done((f32[6,8,1024]{2,1,0:T(8,128)S(1)}, f32[6,8,1024]{2,1,0:T(8,128)S(1)}, u32[]{:S(2)}, u32[]{:S(2)}) %collective-permute-start) | collective-permute-done | bytes 196640 | tf_op jit(solution)/shard_map/while/body/eval_jaxpr/ppermute | solution.py:21
  613.2 14.7 %collective-permute-done = f32[6,8,1024]{2,1,0:T(8,128)S(1)} collective-permute-done((f32[6,8,1024]{2,1,0:T(8,128)S(1)}, f32[6,8,1024]{2,1,0:T(8,128)S(1)}, u32[]{:S(2)}, u32[]{:S(2)}) %collective-permute-start) | collective-permute-done | bytes 196640 | tf_op jit(solution)/shard_map/while/body/eval_jaxpr/ppermute | solution.py:21
  648.1 14.3 %collective-permute-done = f32[6,8,1024]{2,1,0:T(8,128)S(1)} collective-permute-done((f32[6,8,1024]{2,1,0:T(8,128)S(1)}, f32[6,8,1024]{2,1,0:T(8,128)S(1)}, u32[]{:S(2)}, u32[]{:S(2)}) %collective-permute-start) | collective-permute-done | bytes 196640 | tf_op jit(solution)/shard_map/while/body/eval_jaxpr/ppermute | solution.py:21
  751.6 14.3 %collective-permute-done = f32[6,8,1024]{2,1,0:T(8,128)S(1)} collective-permute-done((f32[6,8,1024]{2,1,0:T(8,128)S(1)}, f32[6,8,1024]{2,1,0:T(8,128)S(1)}, u32[]{:S(2)}, u32[]{:S(2)}) %collective-permute-start) | collective-permute-done | bytes 196640 | tf_op jit(solution)/shard_map/while/body/eval_jaxpr/ppermute | solution.py:21
  803.3 14.4 %collective-permute-done = f32[6,8,1024]{2,1,0:T(8,128)S(1)} collective-permute-done((f32[6,8,1024]{2,1,0:T(8,128)S(1)}, f32[6,8,1024]{2,1,0:T(8,128)S(1)}, u32[]{:S(2)}, u32[]{:S(2)}) %collective-permute-start) | collective-permute-done | bytes 196640 | tf_op jit(solution)/shard_map/while/body/eval_jaxpr/ppermute | solution.py:21
  820.6 15.5 %collective-permute-done = f32[6,8,1024]{2,1,0:T(8,128)S(1)} collective-permute-done((f32[6,8,1024]{2,1,0:T(8,128)S(1)}, f32[6,8,1024]{2,1,0:T(8,128)S(1)}, u32[]{:S(2)}, u32[]{:S(2)}) %collective-permute-start) | collective-permute-done | bytes 196640 | tf_op jit(solution)/shard_map/while/body/eval_jaxpr/ppermute | solution.py:21
  839.1 14.3 %collective-permute-done = f32[6,8,1024]{2,1,0:T(8,128)S(1)} collective-permute-done((f32[6,8,1024]{2,1,0:T(8,128)S(1)}, f32[6,8,1024]{2,1,0:T(8,128)S(1)}, u32[]{:S(2)}, u32[]{:S(2)}) %collective-permute-start) | collective-permute-done | bytes 196640 | tf_op jit(solution)/shard_map/while/body/eval_jaxpr/ppermute | solution.py:21
  (181 shorter events, 331.9 us)
Async XLA Ops:
  7.2 242.1 %all-gather.2.cloned.1.call-start = ((), (), s32[]{:S(2)}) async-start(), calls=%async_computation | async-start | bytes 3244032 | tf_op jit(solution)/shard_map/all_gather | solution.py:46
  9.6 247.5 %collective-permute-start.4 = (bf16[128,512]{0,1:T(8,128)(2,1)}, bf16[128,512]{0,1:T(8,128)(2,1)}, u32[]{:S(2)}, u32[]{:S(2)}) collective-permute-start(bf16[128,512]{0,1:T(8,128)(2,1)} %copy.43), channel_id=1, source_target_pairs={{0,8},{8,0},{1,9},{9,1},{2,10},{10,2},{3,11},{11,3},{4,12},{12,4},... | collective-permute-start | bytes 393224 | tf_op jit(solution)/shard_map/ppermute | solution.py:16
  25.3 233.0 %collective-permute-start.3 = (bf16[128,512]{0,1:T(8,128)(2,1)}, bf16[128,512]{0,1:T(8,128)(2,1)}, u32[]{:S(2)}, u32[]{:S(2)}) collective-permute-start(bf16[128,512]{0,1:T(8,128)(2,1)} %copy.43), channel_id=1, source_target_pairs={{0,4},{4,0},{1,5},{5,1},{2,6},{6,2},{3,7},{7,3},{8,12},{12,8},{9,1... | collective-permute-start | bytes 393224 | tf_op jit(solution)/shard_map/ppermute | solution.py:16
  29.5 230.0 %collective-permute-start.2 = (bf16[128,512]{0,1:T(8,128)(2,1)}, bf16[128,512]{0,1:T(8,128)(2,1)}, u32[]{:S(2)}, u32[]{:S(2)}) collective-permute-start(bf16[128,512]{0,1:T(8,128)(2,1)} %copy.43), channel_id=1, source_target_pairs={{0,2},{2,0},{1,3},{3,1},{4,6},{6,4},{5,7},{7,5},{8,10},{10,8},{9,1... | collective-permute-start | bytes 393224 | tf_op jit(solution)/shard_map/ppermute | solution.py:16
  32.8 228.0 %collective-permute-start.1 = (bf16[128,512]{0,1:T(8,128)(2,1)}, bf16[128,512]{0,1:T(8,128)(2,1)}, u32[]{:S(2)}, u32[]{:S(2)}) collective-permute-start(bf16[128,512]{0,1:T(8,128)(2,1)} %copy.43), channel_id=1, source_target_pairs={{0,1},{1,0},{2,3},{3,2},{4,5},{5,4},{6,7},{7,6},{8,9},{9,8},{10,11... | collective-permute-start | bytes 393224 | tf_op jit(solution)/shard_map/ppermute | solution.py:16
  276.4 596.2 %collective-permute-start.8 = (f32[128,512]{0,1:T(8,128)}, f32[128,512]{0,1:T(8,128)S(1)}, u32[]{:S(2)}, u32[]{:S(2)}) collective-permute-start(f32[128,512]{0,1:T(8,128)} %bitcast.26), channel_id=1, source_target_pairs={{0,8},{8,0},{1,9},{9,1},{2,10},{10,2},{3,11},{11,3},{4,12},{12,4},... | collective-permute-start | bytes 786440 | tf_op jit(solution)/shard_map/ppermute | solution.py:16
  282.1 590.6 %collective-permute-start.7 = (f32[128,512]{0,1:T(8,128)}, f32[128,512]{0,1:T(8,128)}, u32[]{:S(2)}, u32[]{:S(2)}) collective-permute-start(f32[128,512]{0,1:T(8,128)} %bitcast.23), channel_id=1, source_target_pairs={{0,4},{4,0},{1,5},{5,1},{2,6},{6,2},{3,7},{7,3},{8,12},{12,8},{9,1... | collective-permute-start | bytes 786440 | tf_op jit(solution)/shard_map/ppermute | solution.py:16
  288.1 584.6 %collective-permute-start.6 = (f32[128,512]{0,1:T(8,128)}, f32[128,512]{0,1:T(8,128)}, u32[]{:S(2)}, u32[]{:S(2)}) collective-permute-start(f32[128,512]{0,1:T(8,128)} %bitcast.20), channel_id=1, source_target_pairs={{0,2},{2,0},{1,3},{3,1},{4,6},{6,4},{5,7},{7,5},{8,10},{10,8},{9,1... | collective-permute-start | bytes 786440 | tf_op jit(solution)/shard_map/ppermute | solution.py:16
  291.4 581.3 %collective-permute-start.5 = (f32[128,512]{0,1:T(8,128)}, f32[128,512]{0,1:T(8,128)}, u32[]{:S(2)}, u32[]{:S(2)}) collective-permute-start(f32[128,512]{0,1:T(8,128)} %bitcast.17), channel_id=1, source_target_pairs={{0,1},{1,0},{2,3},{3,2},{4,5},{5,4},{6,7},{7,6},{8,9},{9,8},{10,11... | collective-permute-start | bytes 786440 | tf_op jit(solution)/shard_map/ppermute | solution.py:16
  328.9 17.9 %collective-permute-start = (f32[6,8,1024]{2,1,0:T(8,128)S(1)}, f32[6,8,1024]{2,1,0:T(8,128)S(1)}, u32[]{:S(2)}, u32[]{:S(2)}) collective-permute-start(f32[6,8,1024]{2,1,0:T(8,128)S(1)} %get-tuple-element.217), channel_id=1, source_target_pairs={{0,16},{16,32},{32,48},{48,64},{64,80},{80,96},{96,112},{112,128},... | collective-permute-start | bytes 589832 | tf_op jit(solution)/shard_map/while/body/eval_jaxpr/ppermute | solution.py:21
  347.7 17.1 %collective-permute-start = (f32[6,8,1024]{2,1,0:T(8,128)S(1)}, f32[6,8,1024]{2,1,0:T(8,128)S(1)}, u32[]{:S(2)}, u32[]{:S(2)}) collective-permute-start(f32[6,8,1024]{2,1,0:T(8,128)S(1)} %get-tuple-element.217), channel_id=1, source_target_pairs={{0,16},{16,32},{32,48},{48,64},{64,80},{80,96},{96,112},{112,128},... | collective-permute-start | bytes 589832 | tf_op jit(solution)/shard_map/while/body/eval_jaxpr/ppermute | solution.py:21
  365.8 16.3 %collective-permute-start = (f32[6,8,1024]{2,1,0:T(8,128)S(1)}, f32[6,8,1024]{2,1,0:T(8,128)S(1)}, u32[]{:S(2)}, u32[]{:S(2)}) collective-permute-start(f32[6,8,1024]{2,1,0:T(8,128)S(1)} %get-tuple-element.217), channel_id=1, source_target_pairs={{0,16},{16,32},{32,48},{48,64},{64,80},{80,96},{96,112},{112,128},... | collective-permute-start | bytes 589832 | tf_op jit(solution)/shard_map/while/body/eval_jaxpr/ppermute | solution.py:21
  383.0 16.3 %collective-permute-start = (f32[6,8,1024]{2,1,0:T(8,128)S(1)}, f32[6,8,1024]{2,1,0:T(8,128)S(1)}, u32[]{:S(2)}, u32[]{:S(2)}) collective-permute-start(f32[6,8,1024]{2,1,0:T(8,128)S(1)} %get-tuple-element.217), channel_id=1, source_target_pairs={{0,16},{16,32},{32,48},{48,64},{64,80},{80,96},{96,112},{112,128},... | collective-permute-start | bytes 589832 | tf_op jit(solution)/shard_map/while/body/eval_jaxpr/ppermute | solution.py:21
  400.3 16.3 %collective-permute-start = (f32[6,8,1024]{2,1,0:T(8,128)S(1)}, f32[6,8,1024]{2,1,0:T(8,128)S(1)}, u32[]{:S(2)}, u32[]{:S(2)}) collective-permute-start(f32[6,8,1024]{2,1,0:T(8,128)S(1)} %get-tuple-element.217), channel_id=1, source_target_pairs={{0,16},{16,32},{32,48},{48,64},{64,80},{80,96},{96,112},{112,128},... | collective-permute-start | bytes 589832 | tf_op jit(solution)/shard_map/while/body/eval_jaxpr/ppermute | solution.py:21
  486.5 16.3 %collective-permute-start = (f32[6,8,1024]{2,1,0:T(8,128)S(1)}, f32[6,8,1024]{2,1,0:T(8,128)S(1)}, u32[]{:S(2)}, u32[]{:S(2)}) collective-permute-start(f32[6,8,1024]{2,1,0:T(8,128)S(1)} %get-tuple-element.217), channel_id=1, source_target_pairs={{0,16},{16,32},{32,48},{48,64},{64,80},{80,96},{96,112},{112,128},... | collective-permute-start | bytes 589832 | tf_op jit(solution)/shard_map/while/body/eval_jaxpr/ppermute | solution.py:21
  503.7 16.3 %collective-permute-start = (f32[6,8,1024]{2,1,0:T(8,128)S(1)}, f32[6,8,1024]{2,1,0:T(8,128)S(1)}, u32[]{:S(2)}, u32[]{:S(2)}) collective-permute-start(f32[6,8,1024]{2,1,0:T(8,128)S(1)} %get-tuple-element.217), channel_id=1, source_target_pairs={{0,16},{16,32},{32,48},{48,64},{64,80},{80,96},{96,112},{112,128},... | collective-permute-start | bytes 589832 | tf_op jit(solution)/shard_map/while/body/eval_jaxpr/ppermute | solution.py:21
  555.5 17.1 %collective-permute-start = (f32[6,8,1024]{2,1,0:T(8,128)S(1)}, f32[6,8,1024]{2,1,0:T(8,128)S(1)}, u32[]{:S(2)}, u32[]{:S(2)}) collective-permute-start(f32[6,8,1024]{2,1,0:T(8,128)S(1)} %get-tuple-element.217), channel_id=1, source_target_pairs={{0,16},{16,32},{32,48},{48,64},{64,80},{80,96},{96,112},{112,128},... | collective-permute-start | bytes 589832 | tf_op jit(solution)/shard_map/while/body/eval_jaxpr/ppermute | solution.py:21
  573.5 18.3 %collective-permute-start = (f32[6,8,1024]{2,1,0:T(8,128)S(1)}, f32[6,8,1024]{2,1,0:T(8,128)S(1)}, u32[]{:S(2)}, u32[]{:S(2)}) collective-permute-start(f32[6,8,1024]{2,1,0:T(8,128)S(1)} %get-tuple-element.217), channel_id=1, source_target_pairs={{0,16},{16,32},{32,48},{48,64},{64,80},{80,96},{96,112},{112,128},... | collective-permute-start | bytes 589832 | tf_op jit(solution)/shard_map/while/body/eval_jaxpr/ppermute | solution.py:21
  592.8 17.5 %collective-permute-start = (f32[6,8,1024]{2,1,0:T(8,128)S(1)}, f32[6,8,1024]{2,1,0:T(8,128)S(1)}, u32[]{:S(2)}, u32[]{:S(2)}) collective-permute-start(f32[6,8,1024]{2,1,0:T(8,128)S(1)} %get-tuple-element.217), channel_id=1, source_target_pairs={{0,16},{16,32},{32,48},{48,64},{64,80},{80,96},{96,112},{112,128},... | collective-permute-start | bytes 589832 | tf_op jit(solution)/shard_map/while/body/eval_jaxpr/ppermute | solution.py:21
  611.3 16.7 %collective-permute-start = (f32[6,8,1024]{2,1,0:T(8,128)S(1)}, f32[6,8,1024]{2,1,0:T(8,128)S(1)}, u32[]{:S(2)}, u32[]{:S(2)}) collective-permute-start(f32[6,8,1024]{2,1,0:T(8,128)S(1)} %get-tuple-element.217), channel_id=1, source_target_pairs={{0,16},{16,32},{32,48},{48,64},{64,80},{80,96},{96,112},{112,128},... | collective-permute-start | bytes 589832 | tf_op jit(solution)/shard_map/while/body/eval_jaxpr/ppermute | solution.py:21
  628.9 16.3 %collective-permute-start = (f32[6,8,1024]{2,1,0:T(8,128)S(1)}, f32[6,8,1024]{2,1,0:T(8,128)S(1)}, u32[]{:S(2)}, u32[]{:S(2)}) collective-permute-start(f32[6,8,1024]{2,1,0:T(8,128)S(1)} %get-tuple-element.217), channel_id=1, source_target_pairs={{0,16},{16,32},{32,48},{48,64},{64,80},{80,96},{96,112},{112,128},... | collective-permute-start | bytes 589832 | tf_op jit(solution)/shard_map/while/body/eval_jaxpr/ppermute | solution.py:21
  646.2 16.3 %collective-permute-start = (f32[6,8,1024]{2,1,0:T(8,128)S(1)}, f32[6,8,1024]{2,1,0:T(8,128)S(1)}, u32[]{:S(2)}, u32[]{:S(2)}) collective-permute-start(f32[6,8,1024]{2,1,0:T(8,128)S(1)} %get-tuple-element.217), channel_id=1, source_target_pairs={{0,16},{16,32},{32,48},{48,64},{64,80},{80,96},{96,112},{112,128},... | collective-permute-start | bytes 589832 | tf_op jit(solution)/shard_map/while/body/eval_jaxpr/ppermute | solution.py:21
  801.4 16.3 %collective-permute-start = (f32[6,8,1024]{2,1,0:T(8,128)S(1)}, f32[6,8,1024]{2,1,0:T(8,128)S(1)}, u32[]{:S(2)}, u32[]{:S(2)}) collective-permute-start(f32[6,8,1024]{2,1,0:T(8,128)S(1)} %get-tuple-element.217), channel_id=1, source_target_pairs={{0,16},{16,32},{32,48},{48,64},{64,80},{80,96},{96,112},{112,128},... | collective-permute-start | bytes 589832 | tf_op jit(solution)/shard_map/while/body/eval_jaxpr/ppermute | solution.py:21
  818.7 17.5 %collective-permute-start = (f32[6,8,1024]{2,1,0:T(8,128)S(1)}, f32[6,8,1024]{2,1,0:T(8,128)S(1)}, u32[]{:S(2)}, u32[]{:S(2)}) collective-permute-start(f32[6,8,1024]{2,1,0:T(8,128)S(1)} %get-tuple-element.217), channel_id=1, source_target_pairs={{0,16},{16,32},{32,48},{48,64},{64,80},{80,96},{96,112},{112,128},... | collective-permute-start | bytes 589832 | tf_op jit(solution)/shard_map/while/body/eval_jaxpr/ppermute | solution.py:21
  (28 other events, 531.0 us)
Sparse Core Ops, SparseCore 0:
  10.1 239.1 all-gather.1
where the time goes:
time: 884 us; the launch traced here: 882 us
  waiting for transfers between devices  662 us (75%)
  starting transfers between devices  102 us (12%)
  local copies, waits for them, and re-layouts  44.5 us (5%)
  other arithmetic  36.4 us (4%)
  matrix products  21 us (2%)
  between operations  14.4 us (2%)
    ppermute x31, waiting for transfers between devices, shifted(): lax.ppermute(value, axis, [(i, (i + by) % devices) for i in range(devices)])  452 us
    all_gather x1, waiting for transfers between devices, body(): weights = lax.all_gather(w_up, 'dp', axis=1, tiled=True)  209 us
    ppermute x31, starting transfers between devices, shifted(): lax.ppermute(value, axis, [(i, (i + by) % devices) for i in range(devices)])  59.5 us
    ppermute x8, starting transfers between devices, partner_2(): return lax.ppermute(block, axis, route)  42.1 us
    add x31, other arithmetic, turn_one(): shifted(carry, 'dp', 1)  29.4 us
    reshape x6, local copies, waits for them, and re-layouts, body(): product_term.reshape(BS, hidden_width) * keep_f[factor][None, :]  18.8 us
  transfers between devices with their start and end apart: 40, of which 32 were waited for; matrix products, arithmetic and copies ran while one was open for 9% of the time, Pallas kernels for 0%

commit v1 on v0

--- a/solution.py
+++ b/solution.py
@@ -43,7 +43,9 @@
     hidden_width = hidden_grad.shape[1]
     local_blocks = local_width // BS
     group_width = hidden_width // local_blocks
-    weights = lax.all_gather(w_up, "dp", axis=1, tiled=True)
+    weights = jnp.concatenate(
+        lax.all_to_all(jnp.stack([w_up] * lax.axis_size("dp")), "dp", 0, 0), axis=1
+    )
     keep_cols = jnp.broadcast_to(pattern[:, :, None], (factor_count, pattern.shape[1], BS)).reshape(
         factor_count, hidden_width
     )

time: 884 us -> 800 us (0.905)
  waiting for transfers between devices: 662 us -> 579 us
  between operations: 14.4 us -> 1.07 us
  starting transfers between devices: 102 us -> 112 us
    all_gather x1 -> x0, waiting for transfers between devices: 209 us -> none  [body(): weights = lax.all_gather(w_up, 'dp', axis=1, tiled=True)]
    all_to_all x0 -> x1, waiting for transfers between devices: none -> 129 us  [body(): lax.all_to_all(jnp.stack([w_up] * lax.axis_size('dp')), 'dp', 0, 0)]
    all_to_all x0 -> x1, starting transfers between devices: none -> 15.4 us  [body(): lax.all_to_all(jnp.stack([w_up] * lax.axis_size('dp')), 'dp', 0, 0)]
  transfers between devices with their start and end apart: 40 -> 40, of which waited for: 32 -> 32; matrix products, arithmetic and copies ran while one was open for 9% -> 10% of each run, Pallas kernels for 0% -> 0%
where the time goes in v1:
time: 800 us; the launch traced here: 797 us
  waiting for transfers between devices  579 us (72%)
  starting transfers between devices  112 us (14%)
  local copies, waits for them, and re-layouts  47 us (6%)
  other arithmetic  34.4 us (4%)
  matrix products  22 us (3%)
    ppermute x31, waiting for transfers between devices, shifted(): lax.ppermute(value, axis, [(i, (i + by) % devices) for i in range(devices)])  451 us
    all_to_all x1, waiting for transfers between devices, body(): lax.all_to_all(jnp.stack([w_up] * lax.axis_size('dp')), 'dp', 0, 0)  129 us
    ppermute x31, starting transfers between devices, shifted(): lax.ppermute(value, axis, [(i, (i + by) % devices) for i in range(devices)])  60.9 us
    ppermute x8, starting transfers between devices, partner_2(): return lax.ppermute(block, axis, route)  35.4 us
    add x31, other arithmetic, turn_one(): shifted(carry, 'dp', 1)  29.4 us
    reshape x6, local copies, waits for them, and re-layouts, body(): product_term.reshape(BS, hidden_width) * keep_f[factor][None, :]  18.8 us
  transfers between devices with their start and end apart: 40, of which 32 were waited for; matrix products, arithmetic and copies ran while one was open for 10% of the time, Pallas kernels for 0%

profile of v1, /device:TPU:8, one launch (start us, length us, event | category | flops | bytes accessed | tf_op | source)
XLA Modules:
  0.0 797.0 jit_solution(855160336017006752)
XLA Ops:
  3.6 15.4 %all-to-all-start = ((bf16[32,6,8,1024]{3,2,1,0:T(8,128)(2,1)}), bf16[32,6,8,1024]{3,2,1,0:T(8,128)(2,1)S(1)}, u32[]{:S(2)}, u32[]{:S(2)}) async-start(bf16[32,6,8,1024]{3,2,1,0:T(8,128)(2,1)} %stack.4), calls=%async_computation | async-start | bytes 6291456 | tf_op jit(solution)/shard_map/all_to_all | solution.py:47
  42.5 128.5 %all-to-all-done = bf16[32,6,8,1024]{3,2,1,0:T(8,128)(2,1)S(1)} async-done(((bf16[32,6,8,1024]{3,2,1,0:T(8,128)(2,1)}), bf16[32,6,8,1024]{3,2,1,0:T(8,128)(2,1)S(1)}, u32[]{:S(2)}, u32[]{:S(2)}) %all-to-all-start) | async-done | bytes 3145760 | tf_op jit(solution)/shard_map/all_to_all | solution.py:47
  251.2 542.7 %while.17 = (s32[]{:T(128)}, f32[6,8,1024]{2,1,0:T(8,128)S(1)}, s32[]{:T(128)}, f32[6,32,8,1024]{3,2,1,0:T(8,128)}, s32[]{:T(128)}, /*index=5*/s32[]{:T(128)}, s32[]{:T(128)}, s32[]{:T(128)}, s32[]{:T(128)}) while((s32[]{:T(128)}, f32[6,8,1024]{2,1,0:T(8,128)S(1)}, s32[]{:T(128)}, f32[6,32,8,1024]{3,2,1,0:T(8,128)}, s32[]{:T(128)}, ...), condition=%wide.region_1.2_spmd, body=%wide.region_0.1_spmd.sunk | while | flops 49170 | bytes 1376560 | solution.py:105
  254.6 14.6 %collective-permute-done = f32[6,8,1024]{2,1,0:T(8,128)S(1)} collective-permute-done((f32[6,8,1024]{2,1,0:T(8,128)S(1)}, f32[6,8,1024]{2,1,0:T(8,128)S(1)}, u32[]{:S(2)}, u32[]{:S(2)}) %collective-permute-start) | collective-permute-done | bytes 196640 | tf_op jit(solution)/shard_map/while/body/eval_jaxpr/ppermute | solution.py:21
  272.0 15.1 %collective-permute-done = f32[6,8,1024]{2,1,0:T(8,128)S(1)} collective-permute-done((f32[6,8,1024]{2,1,0:T(8,128)S(1)}, f32[6,8,1024]{2,1,0:T(8,128)S(1)}, u32[]{:S(2)}, u32[]{:S(2)}) %collective-permute-start) | collective-permute-done | bytes 196640 | tf_op jit(solution)/shard_map/while/body/eval_jaxpr/ppermute | solution.py:21
  290.1 14.3 %collective-permute-done = f32[6,8,1024]{2,1,0:T(8,128)S(1)} collective-permute-done((f32[6,8,1024]{2,1,0:T(8,128)S(1)}, f32[6,8,1024]{2,1,0:T(8,128)S(1)}, u32[]{:S(2)}, u32[]{:S(2)}) %collective-permute-start) | collective-permute-done | bytes 196640 | tf_op jit(solution)/shard_map/while/body/eval_jaxpr/ppermute | solution.py:21
  307.3 14.3 %collective-permute-done = f32[6,8,1024]{2,1,0:T(8,128)S(1)} collective-permute-done((f32[6,8,1024]{2,1,0:T(8,128)S(1)}, f32[6,8,1024]{2,1,0:T(8,128)S(1)}, u32[]{:S(2)}, u32[]{:S(2)}) %collective-permute-start) | collective-permute-done | bytes 196640 | tf_op jit(solution)/shard_map/while/body/eval_jaxpr/ppermute | solution.py:21
  324.6 14.3 %collective-permute-done = f32[6,8,1024]{2,1,0:T(8,128)S(1)} collective-permute-done((f32[6,8,1024]{2,1,0:T(8,128)S(1)}, f32[6,8,1024]{2,1,0:T(8,128)S(1)}, u32[]{:S(2)}, u32[]{:S(2)}) %collective-permute-start) | collective-permute-done | bytes 196640 | tf_op jit(solution)/shard_map/while/body/eval_jaxpr/ppermute | solution.py:21
  341.8 14.3 %collective-permute-done = f32[6,8,1024]{2,1,0:T(8,128)S(1)} collective-permute-done((f32[6,8,1024]{2,1,0:T(8,128)S(1)}, f32[6,8,1024]{2,1,0:T(8,128)S(1)}, u32[]{:S(2)}, u32[]{:S(2)}) %collective-permute-start) | collective-permute-done | bytes 196640 | tf_op jit(solution)/shard_map/while/body/eval_jaxpr/ppermute | solution.py:21
  359.0 14.3 %collective-permute-done = f32[6,8,1024]{2,1,0:T(8,128)S(1)} collective-permute-done((f32[6,8,1024]{2,1,0:T(8,128)S(1)}, f32[6,8,1024]{2,1,0:T(8,128)S(1)}, u32[]{:S(2)}, u32[]{:S(2)}) %collective-permute-start) | collective-permute-done | bytes 196640 | tf_op jit(solution)/shard_map/while/body/eval_jaxpr/ppermute | solution.py:21
  376.3 14.3 %collective-permute-done = f32[6,8,1024]{2,1,0:T(8,128)S(1)} collective-permute-done((f32[6,8,1024]{2,1,0:T(8,128)S(1)}, f32[6,8,1024]{2,1,0:T(8,128)S(1)}, u32[]{:S(2)}, u32[]{:S(2)}) %collective-permute-start) | collective-permute-done | bytes 196640 | tf_op jit(solution)/shard_map/while/body/eval_jaxpr/ppermute | solution.py:21
  393.5 14.3 %collective-permute-done = f32[6,8,1024]{2,1,0:T(8,128)S(1)} collective-permute-done((f32[6,8,1024]{2,1,0:T(8,128)S(1)}, f32[6,8,1024]{2,1,0:T(8,128)S(1)}, u32[]{:S(2)}, u32[]{:S(2)}) %collective-permute-start) | collective-permute-done | bytes 196640 | tf_op jit(solution)/shard_map/while/body/eval_jaxpr/ppermute | solution.py:21
  410.8 14.3 %collective-permute-done = f32[6,8,1024]{2,1,0:T(8,128)S(1)} collective-permute-done((f32[6,8,1024]{2,1,0:T(8,128)S(1)}, f32[6,8,1024]{2,1,0:T(8,128)S(1)}, u32[]{:S(2)}, u32[]{:S(2)}) %collective-permute-start) | collective-permute-done | bytes 196640 | tf_op jit(solution)/shard_map/while/body/eval_jaxpr/ppermute | solution.py:21
  428.0 14.3 %collective-permute-done = f32[6,8,1024]{2,1,0:T(8,128)S(1)} collective-permute-done((f32[6,8,1024]{2,1,0:T(8,128)S(1)}, f32[6,8,1024]{2,1,0:T(8,128)S(1)}, u32[]{:S(2)}, u32[]{:S(2)}) %collective-permute-start) | collective-permute-done | bytes 196640 | tf_op jit(solution)/shard_map/while/body/eval_jaxpr/ppermute | solution.py:21
  445.3 14.3 %collective-permute-done = f32[6,8,1024]{2,1,0:T(8,128)S(1)} collective-permute-done((f32[6,8,1024]{2,1,0:T(8,128)S(1)}, f32[6,8,1024]{2,1,0:T(8,128)S(1)}, u32[]{:S(2)}, u32[]{:S(2)}) %collective-permute-start) | collective-permute-done | bytes 196640 | tf_op jit(solution)/shard_map/while/body/eval_jaxpr/ppermute | solution.py:21
  462.5 14.3 %collective-permute-done = f32[6,8,1024]{2,1,0:T(8,128)S(1)} collective-permute-done((f32[6,8,1024]{2,1,0:T(8,128)S(1)}, f32[6,8,1024]{2,1,0:T(8,128)S(1)}, u32[]{:S(2)}, u32[]{:S(2)}) %collective-permute-start) | collective-permute-done | bytes 196640 | tf_op jit(solution)/shard_map/while/body/eval_jaxpr/ppermute | solution.py:21
  479.8 15.2 %collective-permute-done = f32[6,8,1024]{2,1,0:T(8,128)S(1)} collective-permute-done((f32[6,8,1024]{2,1,0:T(8,128)S(1)}, f32[6,8,1024]{2,1,0:T(8,128)S(1)}, u32[]{:S(2)}, u32[]{:S(2)}) %collective-permute-start) | collective-permute-done | bytes 196640 | tf_op jit(solution)/shard_map/while/body/eval_jaxpr/ppermute | solution.py:21
  497.8 16.3 %collective-permute-done = f32[6,8,1024]{2,1,0:T(8,128)S(1)} collective-permute-done((f32[6,8,1024]{2,1,0:T(8,128)S(1)}, f32[6,8,1024]{2,1,0:T(8,128)S(1)}, u32[]{:S(2)}, u32[]{:S(2)}) %collective-permute-start) | collective-permute-done | bytes 196640 | tf_op jit(solution)/shard_map/while/body/eval_jaxpr/ppermute | solution.py:21
  517.1 15.6 %collective-permute-done = f32[6,8,1024]{2,1,0:T(8,128)S(1)} collective-permute-done((f32[6,8,1024]{2,1,0:T(8,128)S(1)}, f32[6,8,1024]{2,1,0:T(8,128)S(1)}, u32[]{:S(2)}, u32[]{:S(2)}) %collective-permute-start) | collective-permute-done | bytes 196640 | tf_op jit(solution)/shard_map/while/body/eval_jaxpr/ppermute | solution.py:21
  535.6 14.7 %collective-permute-done = f32[6,8,1024]{2,1,0:T(8,128)S(1)} collective-permute-done((f32[6,8,1024]{2,1,0:T(8,128)S(1)}, f32[6,8,1024]{2,1,0:T(8,128)S(1)}, u32[]{:S(2)}, u32[]{:S(2)}) %collective-permute-start) | collective-permute-done | bytes 196640 | tf_op jit(solution)/shard_map/while/body/eval_jaxpr/ppermute | solution.py:21
  553.2 14.3 %collective-permute-done = f32[6,8,1024]{2,1,0:T(8,128)S(1)} collective-permute-done((f32[6,8,1024]{2,1,0:T(8,128)S(1)}, f32[6,8,1024]{2,1,0:T(8,128)S(1)}, u32[]{:S(2)}, u32[]{:S(2)}) %collective-permute-start) | collective-permute-done | bytes 196640 | tf_op jit(solution)/shard_map/while/body/eval_jaxpr/ppermute | solution.py:21
  639.4 14.3 %collective-permute-done = f32[6,8,1024]{2,1,0:T(8,128)S(1)} collective-permute-done((f32[6,8,1024]{2,1,0:T(8,128)S(1)}, f32[6,8,1024]{2,1,0:T(8,128)S(1)}, u32[]{:S(2)}, u32[]{:S(2)}) %collective-permute-start) | collective-permute-done | bytes 196640 | tf_op jit(solution)/shard_map/while/body/eval_jaxpr/ppermute | solution.py:21
  725.7 14.4 %collective-permute-done = f32[6,8,1024]{2,1,0:T(8,128)S(1)} collective-permute-done((f32[6,8,1024]{2,1,0:T(8,128)S(1)}, f32[6,8,1024]{2,1,0:T(8,128)S(1)}, u32[]{:S(2)}, u32[]{:S(2)}) %collective-permute-start) | collective-permute-done | bytes 196640 | tf_op jit(solution)/shard_map/while/body/eval_jaxpr/ppermute | solution.py:21
  743.0 15.5 %collective-permute-done = f32[6,8,1024]{2,1,0:T(8,128)S(1)} collective-permute-done((f32[6,8,1024]{2,1,0:T(8,128)S(1)}, f32[6,8,1024]{2,1,0:T(8,128)S(1)}, u32[]{:S(2)}, u32[]{:S(2)}) %collective-permute-start) | collective-permute-done | bytes 196640 | tf_op jit(solution)/shard_map/while/body/eval_jaxpr/ppermute | solution.py:21
  (181 shorter events, 342.9 us)
Async XLA Ops:
  3.6 167.4 %all-to-all-start = ((bf16[32,6,8,1024]{3,2,1,0:T(8,128)(2,1)}), bf16[32,6,8,1024]{3,2,1,0:T(8,128)(2,1)S(1)}, u32[]{:S(2)}, u32[]{:S(2)}) async-start(bf16[32,6,8,1024]{3,2,1,0:T(8,128)(2,1)} %stack.4), calls=%async_computation | async-start | bytes 6291456 | tf_op jit(solution)/shard_map/all_to_all | solution.py:47
  19.8 158.8 %collective-permute-start.4 = (bf16[128,512]{0,1:T(8,128)(2,1)}, bf16[128,512]{0,1:T(8,128)(2,1)}, u32[]{:S(2)}, u32[]{:S(2)}) collective-permute-start(bf16[128,512]{0,1:T(8,128)(2,1)} %copy.82), channel_id=1, source_target_pairs={{0,8},{8,0},{1,9},{9,1},{2,10},{10,2},{3,11},{11,3},{4,12},{12,4},... | collective-permute-start | bytes 393224 | tf_op jit(solution)/shard_map/ppermute | solution.py:16
  28.0 151.8 %collective-permute-start.3 = (bf16[128,512]{0,1:T(8,128)(2,1)}, bf16[128,512]{0,1:T(8,128)(2,1)}, u32[]{:S(2)}, u32[]{:S(2)}) collective-permute-start(bf16[128,512]{0,1:T(8,128)(2,1)} %copy.82), channel_id=1, source_target_pairs={{0,4},{4,0},{1,5},{5,1},{2,6},{6,2},{3,7},{7,3},{8,12},{12,8},{9,1... | collective-permute-start | bytes 393224 | tf_op jit(solution)/shard_map/ppermute | solution.py:16
  32.2 148.9 %collective-permute-start.2 = (bf16[128,512]{0,1:T(8,128)(2,1)}, bf16[128,512]{0,1:T(8,128)(2,1)}, u32[]{:S(2)}, u32[]{:S(2)}) collective-permute-start(bf16[128,512]{0,1:T(8,128)(2,1)} %copy.82), channel_id=1, source_target_pairs={{0,2},{2,0},{1,3},{3,1},{4,6},{6,4},{5,7},{7,5},{8,10},{10,8},{9,1... | collective-permute-start | bytes 393224 | tf_op jit(solution)/shard_map/ppermute | solution.py:16
  35.5 146.8 %collective-permute-start.1 = (bf16[128,512]{0,1:T(8,128)(2,1)}, bf16[128,512]{0,1:T(8,128)(2,1)}, u32[]{:S(2)}, u32[]{:S(2)}) collective-permute-start(bf16[128,512]{0,1:T(8,128)(2,1)} %copy.82), channel_id=1, source_target_pairs={{0,1},{1,0},{2,3},{3,2},{4,5},{5,4},{6,7},{7,6},{8,9},{9,8},{10,11... | collective-permute-start | bytes 393224 | tf_op jit(solution)/shard_map/ppermute | solution.py:16
  198.0 597.0 %collective-permute-start.8 = (f32[128,512]{0,1:T(8,128)}, f32[128,512]{0,1:T(8,128)S(1)}, u32[]{:S(2)}, u32[]{:S(2)}) collective-permute-start(f32[128,512]{0,1:T(8,128)} %bitcast.28), channel_id=1, source_target_pairs={{0,8},{8,0},{1,9},{9,1},{2,10},{10,2},{3,11},{11,3},{4,12},{12,4},... | collective-permute-start | bytes 786440 | tf_op jit(solution)/shard_map/ppermute | solution.py:16
  206.2 588.8 %collective-permute-start.7 = (f32[128,512]{0,1:T(8,128)}, f32[128,512]{0,1:T(8,128)}, u32[]{:S(2)}, u32[]{:S(2)}) collective-permute-start(f32[128,512]{0,1:T(8,128)} %bitcast.25), channel_id=1, source_target_pairs={{0,4},{4,0},{1,5},{5,1},{2,6},{6,2},{3,7},{7,3},{8,12},{12,8},{9,1... | collective-permute-start | bytes 786440 | tf_op jit(solution)/shard_map/ppermute | solution.py:16
  210.4 584.6 %collective-permute-start.6 = (f32[128,512]{0,1:T(8,128)}, f32[128,512]{0,1:T(8,128)}, u32[]{:S(2)}, u32[]{:S(2)}) collective-permute-start(f32[128,512]{0,1:T(8,128)} %bitcast.22), channel_id=1, source_target_pairs={{0,2},{2,0},{1,3},{3,1},{4,6},{6,4},{5,7},{7,5},{8,10},{10,8},{9,1... | collective-permute-start | bytes 786440 | tf_op jit(solution)/shard_map/ppermute | solution.py:16
  213.7 581.4 %collective-permute-start.5 = (f32[128,512]{0,1:T(8,128)}, f32[128,512]{0,1:T(8,128)}, u32[]{:S(2)}, u32[]{:S(2)}) collective-permute-start(f32[128,512]{0,1:T(8,128)} %bitcast.19), channel_id=1, source_target_pairs={{0,1},{1,0},{2,3},{3,2},{4,5},{5,4},{6,7},{7,6},{8,9},{9,8},{10,11... | collective-permute-start | bytes 786440 | tf_op jit(solution)/shard_map/ppermute | solution.py:16
  251.2 17.9 %collective-permute-start = (f32[6,8,1024]{2,1,0:T(8,128)S(1)}, f32[6,8,1024]{2,1,0:T(8,128)S(1)}, u32[]{:S(2)}, u32[]{:S(2)}) collective-permute-start(f32[6,8,1024]{2,1,0:T(8,128)S(1)} %get-tuple-element.223), channel_id=1, source_target_pairs={{0,16},{16,32},{32,48},{48,64},{64,80},{80,96},{96,112},{112,128},... | collective-permute-start | bytes 589832 | tf_op jit(solution)/shard_map/while/body/eval_jaxpr/ppermute | solution.py:21
  270.1 17.1 %collective-permute-start = (f32[6,8,1024]{2,1,0:T(8,128)S(1)}, f32[6,8,1024]{2,1,0:T(8,128)S(1)}, u32[]{:S(2)}, u32[]{:S(2)}) collective-permute-start(f32[6,8,1024]{2,1,0:T(8,128)S(1)} %get-tuple-element.223), channel_id=1, source_target_pairs={{0,16},{16,32},{32,48},{48,64},{64,80},{80,96},{96,112},{112,128},... | collective-permute-start | bytes 589832 | tf_op jit(solution)/shard_map/while/body/eval_jaxpr/ppermute | solution.py:21
  288.1 16.3 %collective-permute-start = (f32[6,8,1024]{2,1,0:T(8,128)S(1)}, f32[6,8,1024]{2,1,0:T(8,128)S(1)}, u32[]{:S(2)}, u32[]{:S(2)}) collective-permute-start(f32[6,8,1024]{2,1,0:T(8,128)S(1)} %get-tuple-element.223), channel_id=1, source_target_pairs={{0,16},{16,32},{32,48},{48,64},{64,80},{80,96},{96,112},{112,128},... | collective-permute-start | bytes 589832 | tf_op jit(solution)/shard_map/while/body/eval_jaxpr/ppermute | solution.py:21
  305.4 16.3 %collective-permute-start = (f32[6,8,1024]{2,1,0:T(8,128)S(1)}, f32[6,8,1024]{2,1,0:T(8,128)S(1)}, u32[]{:S(2)}, u32[]{:S(2)}) collective-permute-start(f32[6,8,1024]{2,1,0:T(8,128)S(1)} %get-tuple-element.223), channel_id=1, source_target_pairs={{0,16},{16,32},{32,48},{48,64},{64,80},{80,96},{96,112},{112,128},... | collective-permute-start | bytes 589832 | tf_op jit(solution)/shard_map/while/body/eval_jaxpr/ppermute | solution.py:21
  322.6 16.3 %collective-permute-start = (f32[6,8,1024]{2,1,0:T(8,128)S(1)}, f32[6,8,1024]{2,1,0:T(8,128)S(1)}, u32[]{:S(2)}, u32[]{:S(2)}) collective-permute-start(f32[6,8,1024]{2,1,0:T(8,128)S(1)} %get-tuple-element.223), channel_id=1, source_target_pairs={{0,16},{16,32},{32,48},{48,64},{64,80},{80,96},{96,112},{112,128},... | collective-permute-start | bytes 589832 | tf_op jit(solution)/shard_map/while/body/eval_jaxpr/ppermute | solution.py:21
  374.3 16.3 %collective-permute-start = (f32[6,8,1024]{2,1,0:T(8,128)S(1)}, f32[6,8,1024]{2,1,0:T(8,128)S(1)}, u32[]{:S(2)}, u32[]{:S(2)}) collective-permute-start(f32[6,8,1024]{2,1,0:T(8,128)S(1)} %get-tuple-element.223), channel_id=1, source_target_pairs={{0,16},{16,32},{32,48},{48,64},{64,80},{80,96},{96,112},{112,128},... | collective-permute-start | bytes 589832 | tf_op jit(solution)/shard_map/while/body/eval_jaxpr/ppermute | solution.py:21
  391.6 16.3 %collective-permute-start = (f32[6,8,1024]{2,1,0:T(8,128)S(1)}, f32[6,8,1024]{2,1,0:T(8,128)S(1)}, u32[]{:S(2)}, u32[]{:S(2)}) collective-permute-start(f32[6,8,1024]{2,1,0:T(8,128)S(1)} %get-tuple-element.223), channel_id=1, source_target_pairs={{0,16},{16,32},{32,48},{48,64},{64,80},{80,96},{96,112},{112,128},... | collective-permute-start | bytes 589832 | tf_op jit(solution)/shard_map/while/body/eval_jaxpr/ppermute | solution.py:21
  477.8 17.1 %collective-permute-start = (f32[6,8,1024]{2,1,0:T(8,128)S(1)}, f32[6,8,1024]{2,1,0:T(8,128)S(1)}, u32[]{:S(2)}, u32[]{:S(2)}) collective-permute-start(f32[6,8,1024]{2,1,0:T(8,128)S(1)} %get-tuple-element.223), channel_id=1, source_target_pairs={{0,16},{16,32},{32,48},{48,64},{64,80},{80,96},{96,112},{112,128},... | collective-permute-start | bytes 589832 | tf_op jit(solution)/shard_map/while/body/eval_jaxpr/ppermute | solution.py:21
  495.9 18.3 %collective-permute-start = (f32[6,8,1024]{2,1,0:T(8,128)S(1)}, f32[6,8,1024]{2,1,0:T(8,128)S(1)}, u32[]{:S(2)}, u32[]{:S(2)}) collective-permute-start(f32[6,8,1024]{2,1,0:T(8,128)S(1)} %get-tuple-element.223), channel_id=1, source_target_pairs={{0,16},{16,32},{32,48},{48,64},{64,80},{80,96},{96,112},{112,128},... | collective-permute-start | bytes 589832 | tf_op jit(solution)/shard_map/while/body/eval_jaxpr/ppermute | solution.py:21
  515.1 17.5 %collective-permute-start = (f32[6,8,1024]{2,1,0:T(8,128)S(1)}, f32[6,8,1024]{2,1,0:T(8,128)S(1)}, u32[]{:S(2)}, u32[]{:S(2)}) collective-permute-start(f32[6,8,1024]{2,1,0:T(8,128)S(1)} %get-tuple-element.223), channel_id=1, source_target_pairs={{0,16},{16,32},{32,48},{48,64},{64,80},{80,96},{96,112},{112,128},... | collective-permute-start | bytes 589832 | tf_op jit(solution)/shard_map/while/body/eval_jaxpr/ppermute | solution.py:21
  533.6 16.7 %collective-permute-start = (f32[6,8,1024]{2,1,0:T(8,128)S(1)}, f32[6,8,1024]{2,1,0:T(8,128)S(1)}, u32[]{:S(2)}, u32[]{:S(2)}) collective-permute-start(f32[6,8,1024]{2,1,0:T(8,128)S(1)} %get-tuple-element.223), channel_id=1, source_target_pairs={{0,16},{16,32},{32,48},{48,64},{64,80},{80,96},{96,112},{112,128},... | collective-permute-start | bytes 589832 | tf_op jit(solution)/shard_map/while/body/eval_jaxpr/ppermute | solution.py:21
  620.2 16.3 %collective-permute-start = (f32[6,8,1024]{2,1,0:T(8,128)S(1)}, f32[6,8,1024]{2,1,0:T(8,128)S(1)}, u32[]{:S(2)}, u32[]{:S(2)}) collective-permute-start(f32[6,8,1024]{2,1,0:T(8,128)S(1)} %get-tuple-element.223), channel_id=1, source_target_pairs={{0,16},{16,32},{32,48},{48,64},{64,80},{80,96},{96,112},{112,128},... | collective-permute-start | bytes 589832 | tf_op jit(solution)/shard_map/while/body/eval_jaxpr/ppermute | solution.py:21
  637.5 16.3 %collective-permute-start = (f32[6,8,1024]{2,1,0:T(8,128)S(1)}, f32[6,8,1024]{2,1,0:T(8,128)S(1)}, u32[]{:S(2)}, u32[]{:S(2)}) collective-permute-start(f32[6,8,1024]{2,1,0:T(8,128)S(1)} %get-tuple-element.223), channel_id=1, source_target_pairs={{0,16},{16,32},{32,48},{48,64},{64,80},{80,96},{96,112},{112,128},... | collective-permute-start | bytes 589832 | tf_op jit(solution)/shard_map/while/body/eval_jaxpr/ppermute | solution.py:21
  723.7 16.3 %collective-permute-start = (f32[6,8,1024]{2,1,0:T(8,128)S(1)}, f32[6,8,1024]{2,1,0:T(8,128)S(1)}, u32[]{:S(2)}, u32[]{:S(2)}) collective-permute-start(f32[6,8,1024]{2,1,0:T(8,128)S(1)} %get-tuple-element.223), channel_id=1, source_target_pairs={{0,16},{16,32},{32,48},{48,64},{64,80},{80,96},{96,112},{112,128},... | collective-permute-start | bytes 589832 | tf_op jit(solution)/shard_map/while/body/eval_jaxpr/ppermute | solution.py:21
  741.0 17.5 %collective-permute-start = (f32[6,8,1024]{2,1,0:T(8,128)S(1)}, f32[6,8,1024]{2,1,0:T(8,128)S(1)}, u32[]{:S(2)}, u32[]{:S(2)}) collective-permute-start(f32[6,8,1024]{2,1,0:T(8,128)S(1)} %get-tuple-element.223), channel_id=1, source_target_pairs={{0,16},{16,32},{32,48},{48,64},{64,80},{80,96},{96,112},{112,128},... | collective-permute-start | bytes 589832 | tf_op jit(solution)/shard_map/while/body/eval_jaxpr/ppermute | solution.py:21
  (28 other events, 367.7 us)
